TPU v7x, 256 devices: a whole 4x4x8 slice. The times are simulated.
256 devices in a mesh: blk: 32 (over y, x, z_hi), grp: 8 (over z_lo, core).
Axes of the slice: x: 4, y: 4, z: 8 (z_hi: 2, z_lo: 4; z = z_hi * 4 + z_lo), core: 2. Of those that a mesh axis runs over, the one named last changes fastest.
Arguments:
- x_blocks: bfloat16 [4096, 128, 128], P(('blk', 'grp')), may hold values from -0.59765625 to 0.59765625
- pair_left: int32 [32, 8, 32, 12], P('blk', 'grp'), may hold values from 0 to 127
- pair_right: int32 [32, 8, 32, 12], P('blk', 'grp'), may hold values from 0 to 127
- pair_target: int32 [32, 8, 32, 12], P('blk', 'grp'), may hold values from 0 to 3
Outputs:
- c_blocks: bfloat16 [32, 8, 4, 128, 128], P('blk', 'grp')
All inputs are finite; a program needn't handle non-finite values.
Results may differ from a plain program's by a relative error of at most 0.001.
Values may be sent and summed in bfloat16 or wider, within the bound.
No kernel may reach another device: no remote copies, remote signals or barrier semaphores. Data moves between devices by JAX's collectives and lax.ppermute only.
A program may use at most 64 MiB of HBM per device.

v0:
```python
import jax
import jax.numpy as jnp
from jax import lax
from jax.sharding import PartitionSpec as P

CS = 4


def from_behind(block, axis, distance):
    devices = range(lax.axis_size(axis))
    route = [((i - distance) % len(devices), i) for i in devices]
    return lax.ppermute(block, axis, route)


def per_device(x_blocks, pair_left, pair_right, pair_target):
    gathered = lax.all_gather(x_blocks, "grp", axis=0, tiled=True)
    group_count = lax.axis_size("blk")
    left_all = pair_left[0, 0]
    right_all = pair_right[0, 0]
    target_all = pair_target[0, 0]
    block_order = x_blocks.shape[1]
    panel_count = gathered.shape[0]
    pair_count = left_all.shape[1]
    flat_panel = gathered.reshape(panel_count, block_order * block_order)

    def partial_value(turn_index):
        left_index = lax.dynamic_index_in_dim(left_all, turn_index, 0, keepdims=False)
        right_index = lax.dynamic_index_in_dim(right_all, turn_index, 0, keepdims=False)
        target_index = lax.dynamic_index_in_dim(target_all, turn_index, 0, keepdims=False)
        both_index = jnp.concatenate([left_index, right_index])
        one_hot = (both_index[:, None] == jnp.arange(panel_count, dtype=jnp.int32)[None, :]).astype(
            jnp.bfloat16
        )
        picked = jnp.dot(one_hot, flat_panel, preferred_element_type=jnp.float32).astype(
            jnp.bfloat16
        )
        picked = picked.reshape(2 * pair_count, block_order, block_order)
        left_tiles = picked[:pair_count]
        right_tiles = picked[pair_count:]
        product = jnp.einsum(
            "pxy,pxz->pyz", left_tiles, right_tiles, preferred_element_type=jnp.float32
        )
        selector = (target_index[:, None] == jnp.arange(CS, dtype=jnp.int32)[None, :]).astype(
            jnp.float32
        )
        return jnp.einsum("pc,pyz->cyz", selector, product, precision=lax.Precision.HIGHEST)

    def advance(turn_index, carried):
        arrived = from_behind(carried, "blk", 1)
        return arrived + partial_value(turn_index)

    summed = lax.fori_loop(1, group_count, advance, partial_value(0))
    return summed.astype(jnp.bfloat16).reshape(1, 1, CS, block_order, block_order)


def solution(mesh):
    return jax.shard_map(
        per_device,
        mesh=mesh,
        in_specs=(
            P(("blk", "grp"), None, None),
            P("blk", "grp", None, None),
            P("blk", "grp", None, None),
            P("blk", "grp", None, None),
        ),
        out_specs=P("blk", "grp", None, None, None),
        check_vma=False,
    )
```

profile of v0, /device:TPU:120, one launch (start us, length us, event | category | flops | bytes accessed | tf_op | source)
XLA Modules:
  0.0 671.8 jit_solution(15409390500098320005)
XLA Ops:
  11.9 50.7 %all-gather.2.cloned.1.call-done = bf16[128,128,128]{2,1,0:T(8,128)(2,1)} async-done(((bf16[16,128,128]{2,1,0:T(8,128)(2,1)}), bf16[128,128,128]{2,1,0:T(8,128)(2,1)}) %all-gather.2.cloned.1.call-update) | async-done | bytes 4194320 | tf_op jit(solution)/shard_map/all_gather | solution.py:16
  74.3 589.9 %while.15 = (s32[]{:T(128)}, f32[4,128,128]{2,0,1:T(4,128)S(1)}, s32[32,12]{1,0:T(8,128)S(1)}, s32[32,12]{1,0:T(8,128)S(1)}, s32[32,12]{1,0:T(8,128)S(1)}, /*ind...) while((s32[]{:T(128)}, f32[4,128,128]{2,0,1:T(4,128)S(1)}, s32[32,12]{1,0:T(8,128)S(1)}, ...), condition=%wide.region_1.2_spmd, body=%wide.region_0.1_spmd.sunk | while | flops 160894032 | bytes 12583719 | solution.py:52
  80.0 11.3 %collective-permute-done = f32[4,128,128]{2,0,1:T(4,128)S(1)} collective-permute-done((f32[4,128,128]{2,0,1:T(4,128)S(1)}, f32[4,128,128]{2,0,1:T(4,128)S(1)}, u32[]{:S(2)}, u32[]{:S(2)}) %collective-permute-start) | collective-permute-done | bytes 262176 | tf_op jit(solution)/shard_map/while/body/eval_jaxpr/ppermute | solution.py:12
  96.0 15.9 %collective-permute-done = f32[4,128,128]{2,0,1:T(4,128)S(1)} collective-permute-done((f32[4,128,128]{2,0,1:T(4,128)S(1)}, f32[4,128,128]{2,0,1:T(4,128)S(1)}, u32[]{:S(2)}, u32[]{:S(2)}) %collective-permute-start) | collective-permute-done | bytes 262176 | tf_op jit(solution)/shard_map/while/body/eval_jaxpr/ppermute | solution.py:12
  116.6 16.1 %collective-permute-done = f32[4,128,128]{2,0,1:T(4,128)S(1)} collective-permute-done((f32[4,128,128]{2,0,1:T(4,128)S(1)}, f32[4,128,128]{2,0,1:T(4,128)S(1)}, u32[]{:S(2)}, u32[]{:S(2)}) %collective-permute-start) | collective-permute-done | bytes 262176 | tf_op jit(solution)/shard_map/while/body/eval_jaxpr/ppermute | solution.py:12
  137.3 12.8 %collective-permute-done = f32[4,128,128]{2,0,1:T(4,128)S(1)} collective-permute-done((f32[4,128,128]{2,0,1:T(4,128)S(1)}, f32[4,128,128]{2,0,1:T(4,128)S(1)}, u32[]{:S(2)}, u32[]{:S(2)}) %collective-permute-start) | collective-permute-done | bytes 262176 | tf_op jit(solution)/shard_map/while/body/eval_jaxpr/ppermute | solution.py:12
  154.8 17.2 %collective-permute-done = f32[4,128,128]{2,0,1:T(4,128)S(1)} collective-permute-done((f32[4,128,128]{2,0,1:T(4,128)S(1)}, f32[4,128,128]{2,0,1:T(4,128)S(1)}, u32[]{:S(2)}, u32[]{:S(2)}) %collective-permute-start) | collective-permute-done | bytes 262176 | tf_op jit(solution)/shard_map/while/body/eval_jaxpr/ppermute | solution.py:12
  176.6 15.8 %collective-permute-done = f32[4,128,128]{2,0,1:T(4,128)S(1)} collective-permute-done((f32[4,128,128]{2,0,1:T(4,128)S(1)}, f32[4,128,128]{2,0,1:T(4,128)S(1)}, u32[]{:S(2)}, u32[]{:S(2)}) %collective-permute-start) | collective-permute-done | bytes 262176 | tf_op jit(solution)/shard_map/while/body/eval_jaxpr/ppermute | solution.py:12
  197.2 12.8 %collective-permute-done = f32[4,128,128]{2,0,1:T(4,128)S(1)} collective-permute-done((f32[4,128,128]{2,0,1:T(4,128)S(1)}, f32[4,128,128]{2,0,1:T(4,128)S(1)}, u32[]{:S(2)}, u32[]{:S(2)}) %collective-permute-start) | collective-permute-done | bytes 262176 | tf_op jit(solution)/shard_map/while/body/eval_jaxpr/ppermute | solution.py:12
  216.1 15.8 %collective-permute-done = f32[4,128,128]{2,0,1:T(4,128)S(1)} collective-permute-done((f32[4,128,128]{2,0,1:T(4,128)S(1)}, f32[4,128,128]{2,0,1:T(4,128)S(1)}, u32[]{:S(2)}, u32[]{:S(2)}) %collective-permute-start) | collective-permute-done | bytes 262176 | tf_op jit(solution)/shard_map/while/body/eval_jaxpr/ppermute | solution.py:12
  236.5 15.7 %collective-permute-done = f32[4,128,128]{2,0,1:T(4,128)S(1)} collective-permute-done((f32[4,128,128]{2,0,1:T(4,128)S(1)}, f32[4,128,128]{2,0,1:T(4,128)S(1)}, u32[]{:S(2)}, u32[]{:S(2)}) %collective-permute-start) | collective-permute-done | bytes 262176 | tf_op jit(solution)/shard_map/while/body/eval_jaxpr/ppermute | solution.py:12
  257.0 12.8 %collective-permute-done = f32[4,128,128]{2,0,1:T(4,128)S(1)} collective-permute-done((f32[4,128,128]{2,0,1:T(4,128)S(1)}, f32[4,128,128]{2,0,1:T(4,128)S(1)}, u32[]{:S(2)}, u32[]{:S(2)}) %collective-permute-start) | collective-permute-done | bytes 262176 | tf_op jit(solution)/shard_map/while/body/eval_jaxpr/ppermute | solution.py:12
  274.4 17.2 %collective-permute-done = f32[4,128,128]{2,0,1:T(4,128)S(1)} collective-permute-done((f32[4,128,128]{2,0,1:T(4,128)S(1)}, f32[4,128,128]{2,0,1:T(4,128)S(1)}, u32[]{:S(2)}, u32[]{:S(2)}) %collective-permute-start) | collective-permute-done | bytes 262176 | tf_op jit(solution)/shard_map/while/body/eval_jaxpr/ppermute | solution.py:12
  296.3 15.9 %collective-permute-done = f32[4,128,128]{2,0,1:T(4,128)S(1)} collective-permute-done((f32[4,128,128]{2,0,1:T(4,128)S(1)}, f32[4,128,128]{2,0,1:T(4,128)S(1)}, u32[]{:S(2)}, u32[]{:S(2)}) %collective-permute-start) | collective-permute-done | bytes 262176 | tf_op jit(solution)/shard_map/while/body/eval_jaxpr/ppermute | solution.py:12
  316.9 12.7 %collective-permute-done = f32[4,128,128]{2,0,1:T(4,128)S(1)} collective-permute-done((f32[4,128,128]{2,0,1:T(4,128)S(1)}, f32[4,128,128]{2,0,1:T(4,128)S(1)}, u32[]{:S(2)}, u32[]{:S(2)}) %collective-permute-start) | collective-permute-done | bytes 262176 | tf_op jit(solution)/shard_map/while/body/eval_jaxpr/ppermute | solution.py:12
  334.2 17.2 %collective-permute-done = f32[4,128,128]{2,0,1:T(4,128)S(1)} collective-permute-done((f32[4,128,128]{2,0,1:T(4,128)S(1)}, f32[4,128,128]{2,0,1:T(4,128)S(1)}, u32[]{:S(2)}, u32[]{:S(2)}) %collective-permute-start) | collective-permute-done | bytes 262176 | tf_op jit(solution)/shard_map/while/body/eval_jaxpr/ppermute | solution.py:12
  356.1 16.5 %collective-permute-done = f32[4,128,128]{2,0,1:T(4,128)S(1)} collective-permute-done((f32[4,128,128]{2,0,1:T(4,128)S(1)}, f32[4,128,128]{2,0,1:T(4,128)S(1)}, u32[]{:S(2)}, u32[]{:S(2)}) %collective-permute-start) | collective-permute-done | bytes 262176 | tf_op jit(solution)/shard_map/while/body/eval_jaxpr/ppermute | solution.py:12
  377.3 13.3 %collective-permute-done = f32[4,128,128]{2,0,1:T(4,128)S(1)} collective-permute-done((f32[4,128,128]{2,0,1:T(4,128)S(1)}, f32[4,128,128]{2,0,1:T(4,128)S(1)}, u32[]{:S(2)}, u32[]{:S(2)}) %collective-permute-start) | collective-permute-done | bytes 262176 | tf_op jit(solution)/shard_map/while/body/eval_jaxpr/ppermute | solution.py:12
  395.3 17.2 %collective-permute-done = f32[4,128,128]{2,0,1:T(4,128)S(1)} collective-permute-done((f32[4,128,128]{2,0,1:T(4,128)S(1)}, f32[4,128,128]{2,0,1:T(4,128)S(1)}, u32[]{:S(2)}, u32[]{:S(2)}) %collective-permute-start) | collective-permute-done | bytes 262176 | tf_op jit(solution)/shard_map/while/body/eval_jaxpr/ppermute | solution.py:12
  417.2 16.6 %collective-permute-done = f32[4,128,128]{2,0,1:T(4,128)S(1)} collective-permute-done((f32[4,128,128]{2,0,1:T(4,128)S(1)}, f32[4,128,128]{2,0,1:T(4,128)S(1)}, u32[]{:S(2)}, u32[]{:S(2)}) %collective-permute-start) | collective-permute-done | bytes 262176 | tf_op jit(solution)/shard_map/while/body/eval_jaxpr/ppermute | solution.py:12
  438.5 12.8 %collective-permute-done = f32[4,128,128]{2,0,1:T(4,128)S(1)} collective-permute-done((f32[4,128,128]{2,0,1:T(4,128)S(1)}, f32[4,128,128]{2,0,1:T(4,128)S(1)}, u32[]{:S(2)}, u32[]{:S(2)}) %collective-permute-start) | collective-permute-done | bytes 262176 | tf_op jit(solution)/shard_map/while/body/eval_jaxpr/ppermute | solution.py:12
  455.9 16.8 %collective-permute-done = f32[4,128,128]{2,0,1:T(4,128)S(1)} collective-permute-done((f32[4,128,128]{2,0,1:T(4,128)S(1)}, f32[4,128,128]{2,0,1:T(4,128)S(1)}, u32[]{:S(2)}, u32[]{:S(2)}) %collective-permute-start) | collective-permute-done | bytes 262176 | tf_op jit(solution)/shard_map/while/body/eval_jaxpr/ppermute | solution.py:12
  477.4 15.0 %collective-permute-done = f32[4,128,128]{2,0,1:T(4,128)S(1)} collective-permute-done((f32[4,128,128]{2,0,1:T(4,128)S(1)}, f32[4,128,128]{2,0,1:T(4,128)S(1)}, u32[]{:S(2)}, u32[]{:S(2)}) %collective-permute-start) | collective-permute-done | bytes 262176 | tf_op jit(solution)/shard_map/while/body/eval_jaxpr/ppermute | solution.py:12
  497.1 16.7 %collective-permute-done = f32[4,128,128]{2,0,1:T(4,128)S(1)} collective-permute-done((f32[4,128,128]{2,0,1:T(4,128)S(1)}, f32[4,128,128]{2,0,1:T(4,128)S(1)}, u32[]{:S(2)}, u32[]{:S(2)}) %collective-permute-start) | collective-permute-done | bytes 262176 | tf_op jit(solution)/shard_map/while/body/eval_jaxpr/ppermute | solution.py:12
  518.5 16.6 %collective-permute-done = f32[4,128,128]{2,0,1:T(4,128)S(1)} collective-permute-done((f32[4,128,128]{2,0,1:T(4,128)S(1)}, f32[4,128,128]{2,0,1:T(4,128)S(1)}, u32[]{:S(2)}, u32[]{:S(2)}) %collective-permute-start) | collective-permute-done | bytes 262176 | tf_op jit(solution)/shard_map/while/body/eval_jaxpr/ppermute | solution.py:12
  539.9 12.9 %collective-permute-done = f32[4,128,128]{2,0,1:T(4,128)S(1)} collective-permute-done((f32[4,128,128]{2,0,1:T(4,128)S(1)}, f32[4,128,128]{2,0,1:T(4,128)S(1)}, u32[]{:S(2)}, u32[]{:S(2)}) %collective-permute-start) | collective-permute-done | bytes 262176 | tf_op jit(solution)/shard_map/while/body/eval_jaxpr/ppermute | solution.py:12
  557.4 11.7 %collective-permute-done = f32[4,128,128]{2,0,1:T(4,128)S(1)} collective-permute-done((f32[4,128,128]{2,0,1:T(4,128)S(1)}, f32[4,128,128]{2,0,1:T(4,128)S(1)}, u32[]{:S(2)}, u32[]{:S(2)}) %collective-permute-start) | collective-permute-done | bytes 262176 | tf_op jit(solution)/shard_map/while/body/eval_jaxpr/ppermute | solution.py:12
  573.8 11.2 %collective-permute-done = f32[4,128,128]{2,0,1:T(4,128)S(1)} collective-permute-done((f32[4,128,128]{2,0,1:T(4,128)S(1)}, f32[4,128,128]{2,0,1:T(4,128)S(1)}, u32[]{:S(2)}, u32[]{:S(2)}) %collective-permute-start) | collective-permute-done | bytes 262176 | tf_op jit(solution)/shard_map/while/body/eval_jaxpr/ppermute | solution.py:12
  589.7 11.2 %collective-permute-done = f32[4,128,128]{2,0,1:T(4,128)S(1)} collective-permute-done((f32[4,128,128]{2,0,1:T(4,128)S(1)}, f32[4,128,128]{2,0,1:T(4,128)S(1)}, u32[]{:S(2)}, u32[]{:S(2)}) %collective-permute-start) | collective-permute-done | bytes 262176 | tf_op jit(solution)/shard_map/while/body/eval_jaxpr/ppermute | solution.py:12
  605.6 11.4 %collective-permute-done = f32[4,128,128]{2,0,1:T(4,128)S(1)} collective-permute-done((f32[4,128,128]{2,0,1:T(4,128)S(1)}, f32[4,128,128]{2,0,1:T(4,128)S(1)}, u32[]{:S(2)}, u32[]{:S(2)}) %collective-permute-start) | collective-permute-done | bytes 262176 | tf_op jit(solution)/shard_map/while/body/eval_jaxpr/ppermute | solution.py:12
  621.6 11.4 %collective-permute-done = f32[4,128,128]{2,0,1:T(4,128)S(1)} collective-permute-done((f32[4,128,128]{2,0,1:T(4,128)S(1)}, f32[4,128,128]{2,0,1:T(4,128)S(1)}, u32[]{:S(2)}, u32[]{:S(2)}) %collective-permute-start) | collective-permute-done | bytes 262176 | tf_op jit(solution)/shard_map/while/body/eval_jaxpr/ppermute | solution.py:12
  637.7 11.4 %collective-permute-done = f32[4,128,128]{2,0,1:T(4,128)S(1)} collective-permute-done((f32[4,128,128]{2,0,1:T(4,128)S(1)}, f32[4,128,128]{2,0,1:T(4,128)S(1)}, u32[]{:S(2)}, u32[]{:S(2)}) %collective-permute-start) | collective-permute-done | bytes 262176 | tf_op jit(solution)/shard_map/while/body/eval_jaxpr/ppermute | solution.py:12
  (329 shorter events, 173.3 us)
Async XLA Ops:
  6.5 56.0 %all-gather.2.cloned.1.call-start = ((), (), s32[]{:S(2)}) async-start(), calls=%async_computation | async-start | bytes 4718592 | tf_op jit(solution)/shard_map/all_gather | solution.py:16
  74.3 17.0 %collective-permute-start = (f32[4,128,128]{2,0,1:T(4,128)S(1)}, f32[4,128,128]{2,0,1:T(4,128)S(1)}, u32[]{:S(2)}, u32[]{:S(2)}) collective-permute-start(f32[4,128,128]{2,0,1:T(4,128)S(1)} %get-tuple-element.235), channel_id=1, source_target_pairs={{248,0},{0,8},{8,16},{16,24},{24,32},{32,40},{40,48},{48,56},{56,6... | collective-permute-start | bytes 786440 | tf_op jit(solution)/shard_map/while/body/eval_jaxpr/ppermute | solution.py:12
  92.2 19.7 %collective-permute-start = (f32[4,128,128]{2,0,1:T(4,128)S(1)}, f32[4,128,128]{2,0,1:T(4,128)S(1)}, u32[]{:S(2)}, u32[]{:S(2)}) collective-permute-start(f32[4,128,128]{2,0,1:T(4,128)S(1)} %get-tuple-element.235), channel_id=1, source_target_pairs={{248,0},{0,8},{8,16},{16,24},{24,32},{32,40},{40,48},{48,56},{56,6... | collective-permute-start | bytes 786440 | tf_op jit(solution)/shard_map/while/body/eval_jaxpr/ppermute | solution.py:12
  112.8 19.8 %collective-permute-start = (f32[4,128,128]{2,0,1:T(4,128)S(1)}, f32[4,128,128]{2,0,1:T(4,128)S(1)}, u32[]{:S(2)}, u32[]{:S(2)}) collective-permute-start(f32[4,128,128]{2,0,1:T(4,128)S(1)} %get-tuple-element.235), channel_id=1, source_target_pairs={{248,0},{0,8},{8,16},{16,24},{24,32},{32,40},{40,48},{48,56},{56,6... | collective-permute-start | bytes 786440 | tf_op jit(solution)/shard_map/while/body/eval_jaxpr/ppermute | solution.py:12
  133.6 16.6 %collective-permute-start = (f32[4,128,128]{2,0,1:T(4,128)S(1)}, f32[4,128,128]{2,0,1:T(4,128)S(1)}, u32[]{:S(2)}, u32[]{:S(2)}) collective-permute-start(f32[4,128,128]{2,0,1:T(4,128)S(1)} %get-tuple-element.235), channel_id=1, source_target_pairs={{248,0},{0,8},{8,16},{16,24},{24,32},{32,40},{40,48},{48,56},{56,6... | collective-permute-start | bytes 786440 | tf_op jit(solution)/shard_map/while/body/eval_jaxpr/ppermute | solution.py:12
  151.0 20.9 %collective-permute-start = (f32[4,128,128]{2,0,1:T(4,128)S(1)}, f32[4,128,128]{2,0,1:T(4,128)S(1)}, u32[]{:S(2)}, u32[]{:S(2)}) collective-permute-start(f32[4,128,128]{2,0,1:T(4,128)S(1)} %get-tuple-element.235), channel_id=1, source_target_pairs={{248,0},{0,8},{8,16},{16,24},{24,32},{32,40},{40,48},{48,56},{56,6... | collective-permute-start | bytes 786440 | tf_op jit(solution)/shard_map/while/body/eval_jaxpr/ppermute | solution.py:12
  172.9 19.6 %collective-permute-start = (f32[4,128,128]{2,0,1:T(4,128)S(1)}, f32[4,128,128]{2,0,1:T(4,128)S(1)}, u32[]{:S(2)}, u32[]{:S(2)}) collective-permute-start(f32[4,128,128]{2,0,1:T(4,128)S(1)} %get-tuple-element.235), channel_id=1, source_target_pairs={{248,0},{0,8},{8,16},{16,24},{24,32},{32,40},{40,48},{48,56},{56,6... | collective-permute-start | bytes 786440 | tf_op jit(solution)/shard_map/while/body/eval_jaxpr/ppermute | solution.py:12
  193.4 16.5 %collective-permute-start = (f32[4,128,128]{2,0,1:T(4,128)S(1)}, f32[4,128,128]{2,0,1:T(4,128)S(1)}, u32[]{:S(2)}, u32[]{:S(2)}) collective-permute-start(f32[4,128,128]{2,0,1:T(4,128)S(1)} %get-tuple-element.235), channel_id=1, source_target_pairs={{248,0},{0,8},{8,16},{16,24},{24,32},{32,40},{40,48},{48,56},{56,6... | collective-permute-start | bytes 786440 | tf_op jit(solution)/shard_map/while/body/eval_jaxpr/ppermute | solution.py:12
  210.9 21.0 %collective-permute-start = (f32[4,128,128]{2,0,1:T(4,128)S(1)}, f32[4,128,128]{2,0,1:T(4,128)S(1)}, u32[]{:S(2)}, u32[]{:S(2)}) collective-permute-start(f32[4,128,128]{2,0,1:T(4,128)S(1)} %get-tuple-element.235), channel_id=1, source_target_pairs={{248,0},{0,8},{8,16},{16,24},{24,32},{32,40},{40,48},{48,56},{56,6... | collective-permute-start | bytes 786440 | tf_op jit(solution)/shard_map/while/body/eval_jaxpr/ppermute | solution.py:12
  232.8 19.5 %collective-permute-start = (f32[4,128,128]{2,0,1:T(4,128)S(1)}, f32[4,128,128]{2,0,1:T(4,128)S(1)}, u32[]{:S(2)}, u32[]{:S(2)}) collective-permute-start(f32[4,128,128]{2,0,1:T(4,128)S(1)} %get-tuple-element.235), channel_id=1, source_target_pairs={{248,0},{0,8},{8,16},{16,24},{24,32},{32,40},{40,48},{48,56},{56,6... | collective-permute-start | bytes 786440 | tf_op jit(solution)/shard_map/while/body/eval_jaxpr/ppermute | solution.py:12
  253.2 16.5 %collective-permute-start = (f32[4,128,128]{2,0,1:T(4,128)S(1)}, f32[4,128,128]{2,0,1:T(4,128)S(1)}, u32[]{:S(2)}, u32[]{:S(2)}) collective-permute-start(f32[4,128,128]{2,0,1:T(4,128)S(1)} %get-tuple-element.235), channel_id=1, source_target_pairs={{248,0},{0,8},{8,16},{16,24},{24,32},{32,40},{40,48},{48,56},{56,6... | collective-permute-start | bytes 786440 | tf_op jit(solution)/shard_map/while/body/eval_jaxpr/ppermute | solution.py:12
  270.7 20.9 %collective-permute-start = (f32[4,128,128]{2,0,1:T(4,128)S(1)}, f32[4,128,128]{2,0,1:T(4,128)S(1)}, u32[]{:S(2)}, u32[]{:S(2)}) collective-permute-start(f32[4,128,128]{2,0,1:T(4,128)S(1)} %get-tuple-element.235), channel_id=1, source_target_pairs={{248,0},{0,8},{8,16},{16,24},{24,32},{32,40},{40,48},{48,56},{56,6... | collective-permute-start | bytes 786440 | tf_op jit(solution)/shard_map/while/body/eval_jaxpr/ppermute | solution.py:12
  292.5 19.7 %collective-permute-start = (f32[4,128,128]{2,0,1:T(4,128)S(1)}, f32[4,128,128]{2,0,1:T(4,128)S(1)}, u32[]{:S(2)}, u32[]{:S(2)}) collective-permute-start(f32[4,128,128]{2,0,1:T(4,128)S(1)} %get-tuple-element.235), channel_id=1, source_target_pairs={{248,0},{0,8},{8,16},{16,24},{24,32},{32,40},{40,48},{48,56},{56,6... | collective-permute-start | bytes 786440 | tf_op jit(solution)/shard_map/while/body/eval_jaxpr/ppermute | solution.py:12
  313.1 16.5 %collective-permute-start = (f32[4,128,128]{2,0,1:T(4,128)S(1)}, f32[4,128,128]{2,0,1:T(4,128)S(1)}, u32[]{:S(2)}, u32[]{:S(2)}) collective-permute-start(f32[4,128,128]{2,0,1:T(4,128)S(1)} %get-tuple-element.235), channel_id=1, source_target_pairs={{248,0},{0,8},{8,16},{16,24},{24,32},{32,40},{40,48},{48,56},{56,6... | collective-permute-start | bytes 786440 | tf_op jit(solution)/shard_map/while/body/eval_jaxpr/ppermute | solution.py:12
  330.5 20.9 %collective-permute-start = (f32[4,128,128]{2,0,1:T(4,128)S(1)}, f32[4,128,128]{2,0,1:T(4,128)S(1)}, u32[]{:S(2)}, u32[]{:S(2)}) collective-permute-start(f32[4,128,128]{2,0,1:T(4,128)S(1)} %get-tuple-element.235), channel_id=1, source_target_pairs={{248,0},{0,8},{8,16},{16,24},{24,32},{32,40},{40,48},{48,56},{56,6... | collective-permute-start | bytes 786440 | tf_op jit(solution)/shard_map/while/body/eval_jaxpr/ppermute | solution.py:12
  352.4 20.3 %collective-permute-start = (f32[4,128,128]{2,0,1:T(4,128)S(1)}, f32[4,128,128]{2,0,1:T(4,128)S(1)}, u32[]{:S(2)}, u32[]{:S(2)}) collective-permute-start(f32[4,128,128]{2,0,1:T(4,128)S(1)} %get-tuple-element.235), channel_id=1, source_target_pairs={{248,0},{0,8},{8,16},{16,24},{24,32},{32,40},{40,48},{48,56},{56,6... | collective-permute-start | bytes 786440 | tf_op jit(solution)/shard_map/while/body/eval_jaxpr/ppermute | solution.py:12
  373.6 17.1 %collective-permute-start = (f32[4,128,128]{2,0,1:T(4,128)S(1)}, f32[4,128,128]{2,0,1:T(4,128)S(1)}, u32[]{:S(2)}, u32[]{:S(2)}) collective-permute-start(f32[4,128,128]{2,0,1:T(4,128)S(1)} %get-tuple-element.235), channel_id=1, source_target_pairs={{248,0},{0,8},{8,16},{16,24},{24,32},{32,40},{40,48},{48,56},{56,6... | collective-permute-start | bytes 786440 | tf_op jit(solution)/shard_map/while/body/eval_jaxpr/ppermute | solution.py:12
  391.6 20.9 %collective-permute-start = (f32[4,128,128]{2,0,1:T(4,128)S(1)}, f32[4,128,128]{2,0,1:T(4,128)S(1)}, u32[]{:S(2)}, u32[]{:S(2)}) collective-permute-start(f32[4,128,128]{2,0,1:T(4,128)S(1)} %get-tuple-element.235), channel_id=1, source_target_pairs={{248,0},{0,8},{8,16},{16,24},{24,32},{32,40},{40,48},{48,56},{56,6... | collective-permute-start | bytes 786440 | tf_op jit(solution)/shard_map/while/body/eval_jaxpr/ppermute | solution.py:12
  413.4 20.4 %collective-permute-start = (f32[4,128,128]{2,0,1:T(4,128)S(1)}, f32[4,128,128]{2,0,1:T(4,128)S(1)}, u32[]{:S(2)}, u32[]{:S(2)}) collective-permute-start(f32[4,128,128]{2,0,1:T(4,128)S(1)} %get-tuple-element.235), channel_id=1, source_target_pairs={{248,0},{0,8},{8,16},{16,24},{24,32},{32,40},{40,48},{48,56},{56,6... | collective-permute-start | bytes 786440 | tf_op jit(solution)/shard_map/while/body/eval_jaxpr/ppermute | solution.py:12
  434.7 16.5 %collective-permute-start = (f32[4,128,128]{2,0,1:T(4,128)S(1)}, f32[4,128,128]{2,0,1:T(4,128)S(1)}, u32[]{:S(2)}, u32[]{:S(2)}) collective-permute-start(f32[4,128,128]{2,0,1:T(4,128)S(1)} %get-tuple-element.235), channel_id=1, source_target_pairs={{248,0},{0,8},{8,16},{16,24},{24,32},{32,40},{40,48},{48,56},{56,6... | collective-permute-start | bytes 786440 | tf_op jit(solution)/shard_map/while/body/eval_jaxpr/ppermute | solution.py:12
  452.2 20.6 %collective-permute-start = (f32[4,128,128]{2,0,1:T(4,128)S(1)}, f32[4,128,128]{2,0,1:T(4,128)S(1)}, u32[]{:S(2)}, u32[]{:S(2)}) collective-permute-start(f32[4,128,128]{2,0,1:T(4,128)S(1)} %get-tuple-element.235), channel_id=1, source_target_pairs={{248,0},{0,8},{8,16},{16,24},{24,32},{32,40},{40,48},{48,56},{56,6... | collective-permute-start | bytes 786440 | tf_op jit(solution)/shard_map/while/body/eval_jaxpr/ppermute | solution.py:12
  473.7 18.8 %collective-permute-start = (f32[4,128,128]{2,0,1:T(4,128)S(1)}, f32[4,128,128]{2,0,1:T(4,128)S(1)}, u32[]{:S(2)}, u32[]{:S(2)}) collective-permute-start(f32[4,128,128]{2,0,1:T(4,128)S(1)} %get-tuple-element.235), channel_id=1, source_target_pairs={{248,0},{0,8},{8,16},{16,24},{24,32},{32,40},{40,48},{48,56},{56,6... | collective-permute-start | bytes 786440 | tf_op jit(solution)/shard_map/while/body/eval_jaxpr/ppermute | solution.py:12
  493.3 20.5 %collective-permute-start = (f32[4,128,128]{2,0,1:T(4,128)S(1)}, f32[4,128,128]{2,0,1:T(4,128)S(1)}, u32[]{:S(2)}, u32[]{:S(2)}) collective-permute-start(f32[4,128,128]{2,0,1:T(4,128)S(1)} %get-tuple-element.235), channel_id=1, source_target_pairs={{248,0},{0,8},{8,16},{16,24},{24,32},{32,40},{40,48},{48,56},{56,6... | collective-permute-start | bytes 786440 | tf_op jit(solution)/shard_map/while/body/eval_jaxpr/ppermute | solution.py:12
  514.8 20.4 %collective-permute-start = (f32[4,128,128]{2,0,1:T(4,128)S(1)}, f32[4,128,128]{2,0,1:T(4,128)S(1)}, u32[]{:S(2)}, u32[]{:S(2)}) collective-permute-start(f32[4,128,128]{2,0,1:T(4,128)S(1)} %get-tuple-element.235), channel_id=1, source_target_pairs={{248,0},{0,8},{8,16},{16,24},{24,32},{32,40},{40,48},{48,56},{56,6... | collective-permute-start | bytes 786440 | tf_op jit(solution)/shard_map/while/body/eval_jaxpr/ppermute | solution.py:12
  536.1 16.7 %collective-permute-start = (f32[4,128,128]{2,0,1:T(4,128)S(1)}, f32[4,128,128]{2,0,1:T(4,128)S(1)}, u32[]{:S(2)}, u32[]{:S(2)}) collective-permute-start(f32[4,128,128]{2,0,1:T(4,128)S(1)} %get-tuple-element.235), channel_id=1, source_target_pairs={{248,0},{0,8},{8,16},{16,24},{24,32},{32,40},{40,48},{48,56},{56,6... | collective-permute-start | bytes 786440 | tf_op jit(solution)/shard_map/while/body/eval_jaxpr/ppermute | solution.py:12
  553.7 15.5 %collective-permute-start = (f32[4,128,128]{2,0,1:T(4,128)S(1)}, f32[4,128,128]{2,0,1:T(4,128)S(1)}, u32[]{:S(2)}, u32[]{:S(2)}) collective-permute-start(f32[4,128,128]{2,0,1:T(4,128)S(1)} %get-tuple-element.235), channel_id=1, source_target_pairs={{248,0},{0,8},{8,16},{16,24},{24,32},{32,40},{40,48},{48,56},{56,6... | collective-permute-start | bytes 786440 | tf_op jit(solution)/shard_map/while/body/eval_jaxpr/ppermute | solution.py:12
  570.1 15.0 %collective-permute-start = (f32[4,128,128]{2,0,1:T(4,128)S(1)}, f32[4,128,128]{2,0,1:T(4,128)S(1)}, u32[]{:S(2)}, u32[]{:S(2)}) collective-permute-start(f32[4,128,128]{2,0,1:T(4,128)S(1)} %get-tuple-element.235), channel_id=1, source_target_pairs={{248,0},{0,8},{8,16},{16,24},{24,32},{32,40},{40,48},{48,56},{56,6... | collective-permute-start | bytes 786440 | tf_op jit(solution)/shard_map/while/body/eval_jaxpr/ppermute | solution.py:12
  586.0 15.0 %collective-permute-start = (f32[4,128,128]{2,0,1:T(4,128)S(1)}, f32[4,128,128]{2,0,1:T(4,128)S(1)}, u32[]{:S(2)}, u32[]{:S(2)}) collective-permute-start(f32[4,128,128]{2,0,1:T(4,128)S(1)} %get-tuple-element.235), channel_id=1, source_target_pairs={{248,0},{0,8},{8,16},{16,24},{24,32},{32,40},{40,48},{48,56},{56,6... | collective-permute-start | bytes 786440 | tf_op jit(solution)/shard_map/while/body/eval_jaxpr/ppermute | solution.py:12
  601.8 15.1 %collective-permute-start = (f32[4,128,128]{2,0,1:T(4,128)S(1)}, f32[4,128,128]{2,0,1:T(4,128)S(1)}, u32[]{:S(2)}, u32[]{:S(2)}) collective-permute-start(f32[4,128,128]{2,0,1:T(4,128)S(1)} %get-tuple-element.235), channel_id=1, source_target_pairs={{248,0},{0,8},{8,16},{16,24},{24,32},{32,40},{40,48},{48,56},{56,6... | collective-permute-start | bytes 786440 | tf_op jit(solution)/shard_map/while/body/eval_jaxpr/ppermute | solution.py:12
  617.9 15.1 %collective-permute-start = (f32[4,128,128]{2,0,1:T(4,128)S(1)}, f32[4,128,128]{2,0,1:T(4,128)S(1)}, u32[]{:S(2)}, u32[]{:S(2)}) collective-permute-start(f32[4,128,128]{2,0,1:T(4,128)S(1)} %get-tuple-element.235), channel_id=1, source_target_pairs={{248,0},{0,8},{8,16},{16,24},{24,32},{32,40},{40,48},{48,56},{56,6... | collective-permute-start | bytes 786440 | tf_op jit(solution)/shard_map/while/body/eval_jaxpr/ppermute | solution.py:12
  633.9 15.1 %collective-permute-start = (f32[4,128,128]{2,0,1:T(4,128)S(1)}, f32[4,128,128]{2,0,1:T(4,128)S(1)}, u32[]{:S(2)}, u32[]{:S(2)}) collective-permute-start(f32[4,128,128]{2,0,1:T(4,128)S(1)} %get-tuple-element.235), channel_id=1, source_target_pairs={{248,0},{0,8},{8,16},{16,24},{24,32},{32,40},{40,48},{48,56},{56,6... | collective-permute-start | bytes 786440 | tf_op jit(solution)/shard_map/while/body/eval_jaxpr/ppermute | solution.py:12
  650.0 13.4 %collective-permute-start = (f32[4,128,128]{2,0,1:T(4,128)S(1)}, f32[4,128,128]{2,0,1:T(4,128)S(1)}, u32[]{:S(2)}, u32[]{:S(2)}) collective-permute-start(f32[4,128,128]{2,0,1:T(4,128)S(1)} %get-tuple-element.235), channel_id=1, source_target_pairs={{248,0},{0,8},{8,16},{16,24},{24,32},{32,40},{40,48},{48,56},{56,6... | collective-permute-start | bytes 786440 | tf_op jit(solution)/shard_map/while/body/eval_jaxpr/ppermute | solution.py:12
  (1 other events, 7.8 us)
Sparse Core Ops, SparseCore 0:
  9.1 53.4 all-gather.1
where the time goes:
time: 673 us; the launch traced here: 672 us
  waiting for transfers between devices  493 us (73%)
  matrix products  131 us (19%)
  local copies, waits for them, and re-layouts  23.7 us (4%)
  between operations  13.4 us (2%)
    ppermute x31, waiting for transfers between devices, from_behind(): return lax.ppermute(block, axis, route)  441 us
    dot_general x32, matrix products, partial_value(): jnp.dot(one_hot, flat_panel, preferred_element_type=jnp.float32)  91.8 us
    all_gather x1, waiting for transfers between devices, per_device(): gathered = lax.all_gather(x_blocks, 'grp', axis=0, tiled=True)  50.7 us
    dot_general x32, matrix products, partial_value(): jnp.einsum('pc,pyz->cyz', selector, product, precision=lax.Precision.HIGH...  28.9 us
  transfers between devices with their start and end apart: 32, of which 32 were waited for; matrix products, arithmetic and copies ran while one was open for 17% of the time, Pallas kernels for 0%

commit v1 on v0

--- a/solution.py
+++ b/solution.py
@@ -13,7 +13,13 @@
 
 
 def per_device(x_blocks, pair_left, pair_right, pair_target):
-    gathered = lax.all_gather(x_blocks, "grp", axis=0, tiled=True)
+    _post_bands = lambda patch: jnp.concatenate(
+        lax.all_to_all(
+            jnp.stack([patch for _ in range(lax.axis_size("grp"))], axis=0), "grp", 0, 0
+        ),
+        axis=0,
+    )
+    gathered = _post_bands(x_blocks)
     group_count = lax.axis_size("blk")
     left_all = pair_left[0, 0]
     right_all = pair_right[0, 0]

time: 673 us -> 652 us (0.969)
  the two profiles are of different devices: /device:TPU:120 before, /device:TPU:88 now
where the time goes in v1:
time: 652 us; the launch traced here: 651 us
  waiting for transfers between devices  442 us (68%)
  matrix products  133 us (20%)
  starting transfers between devices  46.2 us (7%)
  local copies, waits for them, and re-layouts  24.1 us (4%)
    ppermute x31, waiting for transfers between devices, from_behind(): return lax.ppermute(block, axis, route)  353 us
    dot_general x32, matrix products, partial_value(): jnp.dot(one_hot, flat_panel, preferred_element_type=jnp.float32)  94 us
    all_to_all x1, waiting for transfers between devices, per_device(): lax.all_to_all(jnp.stack([patch for _ in range(lax.axis_size('grp'))], ax...  89.5 us
    ppermute x31, starting transfers between devices, from_behind(): return lax.ppermute(block, axis, route)  40.5 us
    dot_general x32, matrix products, partial_value(): jnp.einsum('pc,pyz->cyz', selector, product, precision=lax.Precision.HIGH...  28.9 us
  transfers between devices with their start and end apart: 32, of which 32 were waited for; matrix products, arithmetic and copies ran while one was open for 17% of the time, Pallas kernels for 0%

profile of v1, /device:TPU:88, one launch (start us, length us, event | category | flops | bytes accessed | tf_op | source)
XLA Modules:
  0.0 650.6 jit_solution(9522943776988197377)
XLA Ops:
  10.9 89.5 %all-to-all-done = bf16[8,16,128,128]{3,2,1,0:T(8,128)(2,1)} async-done(((bf16[8,16,128,128]{3,2,1,0:T(8,128)(2,1)}), bf16[8,16,128,128]{3,2,1,0:T(8,128)(2,1)}, u32[]{:S(2)}, u32[]{:S(2)}) %all-to-all-start) | async-done | bytes 4194336 | tf_op jit(solution)/shard_map/all_to_all | solution.py:17
  100.4 7.7 %copy.29 = bf16[16,8,128,128]{3,1,2,0:T(8,128)(2,1)} copy(bf16[16,8,128,128]{3,2,1,0:T(8,128)(2,1)} %bitcast.16) | data formatting | bytes 8388608
  114.2 535.7 %while.15 = (s32[]{:T(128)}, f32[4,128,128]{2,0,1:T(4,128)S(1)}, s32[32,12]{1,0:T(8,128)S(1)}, s32[32,12]{1,0:T(8,128)S(1)}, s32[32,12]{1,0:T(8,128)S(1)}, /*ind...) while((s32[]{:T(128)}, f32[4,128,128]{2,0,1:T(4,128)S(1)}, s32[32,12]{1,0:T(8,128)S(1)}, ...), condition=%wide.region_1.2_spmd, body=%wide.region_0.1_spmd.sunk | while | flops 160894032 | bytes 12583719 | solution.py:58
  138.1 7.6 %collective-permute-done = f32[4,128,128]{2,0,1:T(4,128)S(1)} collective-permute-done((f32[4,128,128]{2,0,1:T(4,128)S(1)}, f32[4,128,128]{2,0,1:T(4,128)S(1)}, u32[]{:S(2)}, u32[]{:S(2)}) %collective-permute-start) | collective-permute-done | bytes 262176 | tf_op jit(solution)/shard_map/while/body/eval_jaxpr/ppermute | solution.py:12
  150.4 9.7 %collective-permute-done = f32[4,128,128]{2,0,1:T(4,128)S(1)} collective-permute-done((f32[4,128,128]{2,0,1:T(4,128)S(1)}, f32[4,128,128]{2,0,1:T(4,128)S(1)}, u32[]{:S(2)}, u32[]{:S(2)}) %collective-permute-start) | collective-permute-done | bytes 262176 | tf_op jit(solution)/shard_map/while/body/eval_jaxpr/ppermute | solution.py:12
  164.7 9.7 %collective-permute-done = f32[4,128,128]{2,0,1:T(4,128)S(1)} collective-permute-done((f32[4,128,128]{2,0,1:T(4,128)S(1)}, f32[4,128,128]{2,0,1:T(4,128)S(1)}, u32[]{:S(2)}, u32[]{:S(2)}) %collective-permute-start) | collective-permute-done | bytes 262176 | tf_op jit(solution)/shard_map/while/body/eval_jaxpr/ppermute | solution.py:12
  179.1 9.7 %collective-permute-done = f32[4,128,128]{2,0,1:T(4,128)S(1)} collective-permute-done((f32[4,128,128]{2,0,1:T(4,128)S(1)}, f32[4,128,128]{2,0,1:T(4,128)S(1)}, u32[]{:S(2)}, u32[]{:S(2)}) %collective-permute-start) | collective-permute-done | bytes 262176 | tf_op jit(solution)/shard_map/while/body/eval_jaxpr/ppermute | solution.py:12
  193.5 9.7 %collective-permute-done = f32[4,128,128]{2,0,1:T(4,128)S(1)} collective-permute-done((f32[4,128,128]{2,0,1:T(4,128)S(1)}, f32[4,128,128]{2,0,1:T(4,128)S(1)}, u32[]{:S(2)}, u32[]{:S(2)}) %collective-permute-start) | collective-permute-done | bytes 262176 | tf_op jit(solution)/shard_map/while/body/eval_jaxpr/ppermute | solution.py:12
  207.9 9.7 %collective-permute-done = f32[4,128,128]{2,0,1:T(4,128)S(1)} collective-permute-done((f32[4,128,128]{2,0,1:T(4,128)S(1)}, f32[4,128,128]{2,0,1:T(4,128)S(1)}, u32[]{:S(2)}, u32[]{:S(2)}) %collective-permute-start) | collective-permute-done | bytes 262176 | tf_op jit(solution)/shard_map/while/body/eval_jaxpr/ppermute | solution.py:12
  222.3 9.7 %collective-permute-done = f32[4,128,128]{2,0,1:T(4,128)S(1)} collective-permute-done((f32[4,128,128]{2,0,1:T(4,128)S(1)}, f32[4,128,128]{2,0,1:T(4,128)S(1)}, u32[]{:S(2)}, u32[]{:S(2)}) %collective-permute-start) | collective-permute-done | bytes 262176 | tf_op jit(solution)/shard_map/while/body/eval_jaxpr/ppermute | solution.py:12
  236.7 9.7 %collective-permute-done = f32[4,128,128]{2,0,1:T(4,128)S(1)} collective-permute-done((f32[4,128,128]{2,0,1:T(4,128)S(1)}, f32[4,128,128]{2,0,1:T(4,128)S(1)}, u32[]{:S(2)}, u32[]{:S(2)}) %collective-permute-start) | collective-permute-done | bytes 262176 | tf_op jit(solution)/shard_map/while/body/eval_jaxpr/ppermute | solution.py:12
  251.1 9.7 %collective-permute-done = f32[4,128,128]{2,0,1:T(4,128)S(1)} collective-permute-done((f32[4,128,128]{2,0,1:T(4,128)S(1)}, f32[4,128,128]{2,0,1:T(4,128)S(1)}, u32[]{:S(2)}, u32[]{:S(2)}) %collective-permute-start) | collective-permute-done | bytes 262176 | tf_op jit(solution)/shard_map/while/body/eval_jaxpr/ppermute | solution.py:12
  289.3 9.8 %collective-permute-done = f32[4,128,128]{2,0,1:T(4,128)S(1)} collective-permute-done((f32[4,128,128]{2,0,1:T(4,128)S(1)}, f32[4,128,128]{2,0,1:T(4,128)S(1)}, u32[]{:S(2)}, u32[]{:S(2)}) %collective-permute-start) | collective-permute-done | bytes 262176 | tf_op jit(solution)/shard_map/while/body/eval_jaxpr/ppermute | solution.py:12
  300.0 9.9 %collective-permute-start = (f32[4,128,128]{2,0,1:T(4,128)S(1)}, f32[4,128,128]{2,0,1:T(4,128)S(1)}, u32[]{:S(2)}, u32[]{:S(2)}) collective-permute-start(f32[4,128,128]{2,0,1:T(4,128)S(1)} %get-tuple-element.235), channel_id=1, source_target_pairs={{248,0},{0,8},{8,16},{16,24},{24,32},{32,40},{40,48},{48,56},{56,6... | collective-permute-start | bytes 786440 | tf_op jit(solution)/shard_map/while/body/eval_jaxpr/ppermute | solution.py:12
  328.3 8.8 %collective-permute-done = f32[4,128,128]{2,0,1:T(4,128)S(1)} collective-permute-done((f32[4,128,128]{2,0,1:T(4,128)S(1)}, f32[4,128,128]{2,0,1:T(4,128)S(1)}, u32[]{:S(2)}, u32[]{:S(2)}) %collective-permute-start) | collective-permute-done | bytes 262176 | tf_op jit(solution)/shard_map/while/body/eval_jaxpr/ppermute | solution.py:12
  341.7 16.4 %collective-permute-done = f32[4,128,128]{2,0,1:T(4,128)S(1)} collective-permute-done((f32[4,128,128]{2,0,1:T(4,128)S(1)}, f32[4,128,128]{2,0,1:T(4,128)S(1)}, u32[]{:S(2)}, u32[]{:S(2)}) %collective-permute-start) | collective-permute-done | bytes 262176 | tf_op jit(solution)/shard_map/while/body/eval_jaxpr/ppermute | solution.py:12
  362.8 13.2 %collective-permute-done = f32[4,128,128]{2,0,1:T(4,128)S(1)} collective-permute-done((f32[4,128,128]{2,0,1:T(4,128)S(1)}, f32[4,128,128]{2,0,1:T(4,128)S(1)}, u32[]{:S(2)}, u32[]{:S(2)}) %collective-permute-start) | collective-permute-done | bytes 262176 | tf_op jit(solution)/shard_map/while/body/eval_jaxpr/ppermute | solution.py:12
  380.7 17.1 %collective-permute-done = f32[4,128,128]{2,0,1:T(4,128)S(1)} collective-permute-done((f32[4,128,128]{2,0,1:T(4,128)S(1)}, f32[4,128,128]{2,0,1:T(4,128)S(1)}, u32[]{:S(2)}, u32[]{:S(2)}) %collective-permute-start) | collective-permute-done | bytes 262176 | tf_op jit(solution)/shard_map/while/body/eval_jaxpr/ppermute | solution.py:12
  402.5 16.4 %collective-permute-done = f32[4,128,128]{2,0,1:T(4,128)S(1)} collective-permute-done((f32[4,128,128]{2,0,1:T(4,128)S(1)}, f32[4,128,128]{2,0,1:T(4,128)S(1)}, u32[]{:S(2)}, u32[]{:S(2)}) %collective-permute-start) | collective-permute-done | bytes 262176 | tf_op jit(solution)/shard_map/while/body/eval_jaxpr/ppermute | solution.py:12
  423.6 12.9 %collective-permute-done = f32[4,128,128]{2,0,1:T(4,128)S(1)} collective-permute-done((f32[4,128,128]{2,0,1:T(4,128)S(1)}, f32[4,128,128]{2,0,1:T(4,128)S(1)}, u32[]{:S(2)}, u32[]{:S(2)}) %collective-permute-start) | collective-permute-done | bytes 262176 | tf_op jit(solution)/shard_map/while/body/eval_jaxpr/ppermute | solution.py:12
  441.1 17.1 %collective-permute-done = f32[4,128,128]{2,0,1:T(4,128)S(1)} collective-permute-done((f32[4,128,128]{2,0,1:T(4,128)S(1)}, f32[4,128,128]{2,0,1:T(4,128)S(1)}, u32[]{:S(2)}, u32[]{:S(2)}) %collective-permute-start) | collective-permute-done | bytes 262176 | tf_op jit(solution)/shard_map/while/body/eval_jaxpr/ppermute | solution.py:12
  462.9 14.6 %collective-permute-done = f32[4,128,128]{2,0,1:T(4,128)S(1)} collective-permute-done((f32[4,128,128]{2,0,1:T(4,128)S(1)}, f32[4,128,128]{2,0,1:T(4,128)S(1)}, u32[]{:S(2)}, u32[]{:S(2)}) %collective-permute-start) | collective-permute-done | bytes 262176 | tf_op jit(solution)/shard_map/while/body/eval_jaxpr/ppermute | solution.py:12
  482.2 11.4 %collective-permute-done = f32[4,128,128]{2,0,1:T(4,128)S(1)} collective-permute-done((f32[4,128,128]{2,0,1:T(4,128)S(1)}, f32[4,128,128]{2,0,1:T(4,128)S(1)}, u32[]{:S(2)}, u32[]{:S(2)}) %collective-permute-start) | collective-permute-done | bytes 262176 | tf_op jit(solution)/shard_map/while/body/eval_jaxpr/ppermute | solution.py:12
  498.3 16.9 %collective-permute-done = f32[4,128,128]{2,0,1:T(4,128)S(1)} collective-permute-done((f32[4,128,128]{2,0,1:T(4,128)S(1)}, f32[4,128,128]{2,0,1:T(4,128)S(1)}, u32[]{:S(2)}, u32[]{:S(2)}) %collective-permute-start) | collective-permute-done | bytes 262176 | tf_op jit(solution)/shard_map/while/body/eval_jaxpr/ppermute | solution.py:12
  519.9 15.1 %collective-permute-done = f32[4,128,128]{2,0,1:T(4,128)S(1)} collective-permute-done((f32[4,128,128]{2,0,1:T(4,128)S(1)}, f32[4,128,128]{2,0,1:T(4,128)S(1)}, u32[]{:S(2)}, u32[]{:S(2)}) %collective-permute-start) | collective-permute-done | bytes 262176 | tf_op jit(solution)/shard_map/while/body/eval_jaxpr/ppermute | solution.py:12
  539.7 14.3 %collective-permute-done = f32[4,128,128]{2,0,1:T(4,128)S(1)} collective-permute-done((f32[4,128,128]{2,0,1:T(4,128)S(1)}, f32[4,128,128]{2,0,1:T(4,128)S(1)}, u32[]{:S(2)}, u32[]{:S(2)}) %collective-permute-start) | collective-permute-done | bytes 262176 | tf_op jit(solution)/shard_map/while/body/eval_jaxpr/ppermute | solution.py:12
  558.7 16.2 %collective-permute-done = f32[4,128,128]{2,0,1:T(4,128)S(1)} collective-permute-done((f32[4,128,128]{2,0,1:T(4,128)S(1)}, f32[4,128,128]{2,0,1:T(4,128)S(1)}, u32[]{:S(2)}, u32[]{:S(2)}) %collective-permute-start) | collective-permute-done | bytes 262176 | tf_op jit(solution)/shard_map/while/body/eval_jaxpr/ppermute | solution.py:12
  579.6 12.2 %collective-permute-done = f32[4,128,128]{2,0,1:T(4,128)S(1)} collective-permute-done((f32[4,128,128]{2,0,1:T(4,128)S(1)}, f32[4,128,128]{2,0,1:T(4,128)S(1)}, u32[]{:S(2)}, u32[]{:S(2)}) %collective-permute-start) | collective-permute-done | bytes 262176 | tf_op jit(solution)/shard_map/while/body/eval_jaxpr/ppermute | solution.py:12
  596.4 9.6 %collective-permute-done = f32[4,128,128]{2,0,1:T(4,128)S(1)} collective-permute-done((f32[4,128,128]{2,0,1:T(4,128)S(1)}, f32[4,128,128]{2,0,1:T(4,128)S(1)}, u32[]{:S(2)}, u32[]{:S(2)}) %collective-permute-start) | collective-permute-done | bytes 262176 | tf_op jit(solution)/shard_map/while/body/eval_jaxpr/ppermute | solution.py:12
  610.8 9.6 %collective-permute-done = f32[4,128,128]{2,0,1:T(4,128)S(1)} collective-permute-done((f32[4,128,128]{2,0,1:T(4,128)S(1)}, f32[4,128,128]{2,0,1:T(4,128)S(1)}, u32[]{:S(2)}, u32[]{:S(2)}) %collective-permute-start) | collective-permute-done | bytes 262176 | tf_op jit(solution)/shard_map/while/body/eval_jaxpr/ppermute | solution.py:12
  625.1 9.6 %collective-permute-done = f32[4,128,128]{2,0,1:T(4,128)S(1)} collective-permute-done((f32[4,128,128]{2,0,1:T(4,128)S(1)}, f32[4,128,128]{2,0,1:T(4,128)S(1)}, u32[]{:S(2)}, u32[]{:S(2)}) %collective-permute-start) | collective-permute-done | bytes 262176 | tf_op jit(solution)/shard_map/while/body/eval_jaxpr/ppermute | solution.py:12
  639.4 9.6 %collective-permute-done = f32[4,128,128]{2,0,1:T(4,128)S(1)} collective-permute-done((f32[4,128,128]{2,0,1:T(4,128)S(1)}, f32[4,128,128]{2,0,1:T(4,128)S(1)}, u32[]{:S(2)}, u32[]{:S(2)}) %collective-permute-start) | collective-permute-done | bytes 262176 | tf_op jit(solution)/shard_map/while/body/eval_jaxpr/ppermute | solution.py:12
  (333 shorter events, 205.0 us)
Async XLA Ops:
  4.0 96.4 %all-to-all-start = ((bf16[8,16,128,128]{3,2,1,0:T(8,128)(2,1)}), bf16[8,16,128,128]{3,2,1,0:T(8,128)(2,1)}, u32[]{:S(2)}, u32[]{:S(2)}) async-start(bf16[8,16,128,128]{3,2,1,0:T(8,128)(2,1)} %stack.2), calls=%async_computation | async-start | bytes 8388608 | tf_op jit(solution)/shard_map/all_to_all | solution.py:17
  114.2 16.7 %collective-permute-start = (f32[4,128,128]{2,0,1:T(4,128)S(1)}, f32[4,128,128]{2,0,1:T(4,128)S(1)}, u32[]{:S(2)}, u32[]{:S(2)}) collective-permute-start(f32[4,128,128]{2,0,1:T(4,128)S(1)} %get-tuple-element.235), channel_id=1, source_target_pairs={{248,0},{0,8},{8,16},{16,24},{24,32},{32,40},{40,48},{48,56},{56,6... | collective-permute-start | bytes 786440 | tf_op jit(solution)/shard_map/while/body/eval_jaxpr/ppermute | solution.py:12
  131.8 13.8 %collective-permute-start = (f32[4,128,128]{2,0,1:T(4,128)S(1)}, f32[4,128,128]{2,0,1:T(4,128)S(1)}, u32[]{:S(2)}, u32[]{:S(2)}) collective-permute-start(f32[4,128,128]{2,0,1:T(4,128)S(1)} %get-tuple-element.235), channel_id=1, source_target_pairs={{248,0},{0,8},{8,16},{16,24},{24,32},{32,40},{40,48},{48,56},{56,6... | collective-permute-start | bytes 786440 | tf_op jit(solution)/shard_map/while/body/eval_jaxpr/ppermute | solution.py:12
  146.6 13.5 %collective-permute-start = (f32[4,128,128]{2,0,1:T(4,128)S(1)}, f32[4,128,128]{2,0,1:T(4,128)S(1)}, u32[]{:S(2)}, u32[]{:S(2)}) collective-permute-start(f32[4,128,128]{2,0,1:T(4,128)S(1)} %get-tuple-element.235), channel_id=1, source_target_pairs={{248,0},{0,8},{8,16},{16,24},{24,32},{32,40},{40,48},{48,56},{56,6... | collective-permute-start | bytes 786440 | tf_op jit(solution)/shard_map/while/body/eval_jaxpr/ppermute | solution.py:12
  161.0 13.5 %collective-permute-start = (f32[4,128,128]{2,0,1:T(4,128)S(1)}, f32[4,128,128]{2,0,1:T(4,128)S(1)}, u32[]{:S(2)}, u32[]{:S(2)}) collective-permute-start(f32[4,128,128]{2,0,1:T(4,128)S(1)} %get-tuple-element.235), channel_id=1, source_target_pairs={{248,0},{0,8},{8,16},{16,24},{24,32},{32,40},{40,48},{48,56},{56,6... | collective-permute-start | bytes 786440 | tf_op jit(solution)/shard_map/while/body/eval_jaxpr/ppermute | solution.py:12
  175.4 13.5 %collective-permute-start = (f32[4,128,128]{2,0,1:T(4,128)S(1)}, f32[4,128,128]{2,0,1:T(4,128)S(1)}, u32[]{:S(2)}, u32[]{:S(2)}) collective-permute-start(f32[4,128,128]{2,0,1:T(4,128)S(1)} %get-tuple-element.235), channel_id=1, source_target_pairs={{248,0},{0,8},{8,16},{16,24},{24,32},{32,40},{40,48},{48,56},{56,6... | collective-permute-start | bytes 786440 | tf_op jit(solution)/shard_map/while/body/eval_jaxpr/ppermute | solution.py:12
  189.7 13.5 %collective-permute-start = (f32[4,128,128]{2,0,1:T(4,128)S(1)}, f32[4,128,128]{2,0,1:T(4,128)S(1)}, u32[]{:S(2)}, u32[]{:S(2)}) collective-permute-start(f32[4,128,128]{2,0,1:T(4,128)S(1)} %get-tuple-element.235), channel_id=1, source_target_pairs={{248,0},{0,8},{8,16},{16,24},{24,32},{32,40},{40,48},{48,56},{56,6... | collective-permute-start | bytes 786440 | tf_op jit(solution)/shard_map/while/body/eval_jaxpr/ppermute | solution.py:12
  204.1 13.5 %collective-permute-start = (f32[4,128,128]{2,0,1:T(4,128)S(1)}, f32[4,128,128]{2,0,1:T(4,128)S(1)}, u32[]{:S(2)}, u32[]{:S(2)}) collective-permute-start(f32[4,128,128]{2,0,1:T(4,128)S(1)} %get-tuple-element.235), channel_id=1, source_target_pairs={{248,0},{0,8},{8,16},{16,24},{24,32},{32,40},{40,48},{48,56},{56,6... | collective-permute-start | bytes 786440 | tf_op jit(solution)/shard_map/while/body/eval_jaxpr/ppermute | solution.py:12
  218.5 13.5 %collective-permute-start = (f32[4,128,128]{2,0,1:T(4,128)S(1)}, f32[4,128,128]{2,0,1:T(4,128)S(1)}, u32[]{:S(2)}, u32[]{:S(2)}) collective-permute-start(f32[4,128,128]{2,0,1:T(4,128)S(1)} %get-tuple-element.235), channel_id=1, source_target_pairs={{248,0},{0,8},{8,16},{16,24},{24,32},{32,40},{40,48},{48,56},{56,6... | collective-permute-start | bytes 786440 | tf_op jit(solution)/shard_map/while/body/eval_jaxpr/ppermute | solution.py:12
  232.9 13.5 %collective-permute-start = (f32[4,128,128]{2,0,1:T(4,128)S(1)}, f32[4,128,128]{2,0,1:T(4,128)S(1)}, u32[]{:S(2)}, u32[]{:S(2)}) collective-permute-start(f32[4,128,128]{2,0,1:T(4,128)S(1)} %get-tuple-element.235), channel_id=1, source_target_pairs={{248,0},{0,8},{8,16},{16,24},{24,32},{32,40},{40,48},{48,56},{56,6... | collective-permute-start | bytes 786440 | tf_op jit(solution)/shard_map/while/body/eval_jaxpr/ppermute | solution.py:12
  247.3 13.5 %collective-permute-start = (f32[4,128,128]{2,0,1:T(4,128)S(1)}, f32[4,128,128]{2,0,1:T(4,128)S(1)}, u32[]{:S(2)}, u32[]{:S(2)}) collective-permute-start(f32[4,128,128]{2,0,1:T(4,128)S(1)} %get-tuple-element.235), channel_id=1, source_target_pairs={{248,0},{0,8},{8,16},{16,24},{24,32},{32,40},{40,48},{48,56},{56,6... | collective-permute-start | bytes 786440 | tf_op jit(solution)/shard_map/while/body/eval_jaxpr/ppermute | solution.py:12
  261.7 16.4 %collective-permute-start = (f32[4,128,128]{2,0,1:T(4,128)S(1)}, f32[4,128,128]{2,0,1:T(4,128)S(1)}, u32[]{:S(2)}, u32[]{:S(2)}) collective-permute-start(f32[4,128,128]{2,0,1:T(4,128)S(1)} %get-tuple-element.235), channel_id=1, source_target_pairs={{248,0},{0,8},{8,16},{16,24},{24,32},{32,40},{40,48},{48,56},{56,6... | collective-permute-start | bytes 786440 | tf_op jit(solution)/shard_map/while/body/eval_jaxpr/ppermute | solution.py:12
  279.1 20.0 %collective-permute-start = (f32[4,128,128]{2,0,1:T(4,128)S(1)}, f32[4,128,128]{2,0,1:T(4,128)S(1)}, u32[]{:S(2)}, u32[]{:S(2)}) collective-permute-start(f32[4,128,128]{2,0,1:T(4,128)S(1)} %get-tuple-element.235), channel_id=1, source_target_pairs={{248,0},{0,8},{8,16},{16,24},{24,32},{32,40},{40,48},{48,56},{56,6... | collective-permute-start | bytes 786440 | tf_op jit(solution)/shard_map/while/body/eval_jaxpr/ppermute | solution.py:12
  300.0 17.2 %collective-permute-start = (f32[4,128,128]{2,0,1:T(4,128)S(1)}, f32[4,128,128]{2,0,1:T(4,128)S(1)}, u32[]{:S(2)}, u32[]{:S(2)}) collective-permute-start(f32[4,128,128]{2,0,1:T(4,128)S(1)} %get-tuple-element.235), channel_id=1, source_target_pairs={{248,0},{0,8},{8,16},{16,24},{24,32},{32,40},{40,48},{48,56},{56,6... | collective-permute-start | bytes 786440 | tf_op jit(solution)/shard_map/while/body/eval_jaxpr/ppermute | solution.py:12
  318.1 19.0 %collective-permute-start = (f32[4,128,128]{2,0,1:T(4,128)S(1)}, f32[4,128,128]{2,0,1:T(4,128)S(1)}, u32[]{:S(2)}, u32[]{:S(2)}) collective-permute-start(f32[4,128,128]{2,0,1:T(4,128)S(1)} %get-tuple-element.235), channel_id=1, source_target_pairs={{248,0},{0,8},{8,16},{16,24},{24,32},{32,40},{40,48},{48,56},{56,6... | collective-permute-start | bytes 786440 | tf_op jit(solution)/shard_map/while/body/eval_jaxpr/ppermute | solution.py:12
  338.0 20.2 %collective-permute-start = (f32[4,128,128]{2,0,1:T(4,128)S(1)}, f32[4,128,128]{2,0,1:T(4,128)S(1)}, u32[]{:S(2)}, u32[]{:S(2)}) collective-permute-start(f32[4,128,128]{2,0,1:T(4,128)S(1)} %get-tuple-element.235), channel_id=1, source_target_pairs={{248,0},{0,8},{8,16},{16,24},{24,32},{32,40},{40,48},{48,56},{56,6... | collective-permute-start | bytes 786440 | tf_op jit(solution)/shard_map/while/body/eval_jaxpr/ppermute | solution.py:12
  359.1 17.0 %collective-permute-start = (f32[4,128,128]{2,0,1:T(4,128)S(1)}, f32[4,128,128]{2,0,1:T(4,128)S(1)}, u32[]{:S(2)}, u32[]{:S(2)}) collective-permute-start(f32[4,128,128]{2,0,1:T(4,128)S(1)} %get-tuple-element.235), channel_id=1, source_target_pairs={{248,0},{0,8},{8,16},{16,24},{24,32},{32,40},{40,48},{48,56},{56,6... | collective-permute-start | bytes 786440 | tf_op jit(solution)/shard_map/while/body/eval_jaxpr/ppermute | solution.py:12
  377.0 20.9 %collective-permute-start = (f32[4,128,128]{2,0,1:T(4,128)S(1)}, f32[4,128,128]{2,0,1:T(4,128)S(1)}, u32[]{:S(2)}, u32[]{:S(2)}) collective-permute-start(f32[4,128,128]{2,0,1:T(4,128)S(1)} %get-tuple-element.235), channel_id=1, source_target_pairs={{248,0},{0,8},{8,16},{16,24},{24,32},{32,40},{40,48},{48,56},{56,6... | collective-permute-start | bytes 786440 | tf_op jit(solution)/shard_map/while/body/eval_jaxpr/ppermute | solution.py:12
  398.7 20.2 %collective-permute-start = (f32[4,128,128]{2,0,1:T(4,128)S(1)}, f32[4,128,128]{2,0,1:T(4,128)S(1)}, u32[]{:S(2)}, u32[]{:S(2)}) collective-permute-start(f32[4,128,128]{2,0,1:T(4,128)S(1)} %get-tuple-element.235), channel_id=1, source_target_pairs={{248,0},{0,8},{8,16},{16,24},{24,32},{32,40},{40,48},{48,56},{56,6... | collective-permute-start | bytes 786440 | tf_op jit(solution)/shard_map/while/body/eval_jaxpr/ppermute | solution.py:12
  419.8 16.6 %collective-permute-start = (f32[4,128,128]{2,0,1:T(4,128)S(1)}, f32[4,128,128]{2,0,1:T(4,128)S(1)}, u32[]{:S(2)}, u32[]{:S(2)}) collective-permute-start(f32[4,128,128]{2,0,1:T(4,128)S(1)} %get-tuple-element.235), channel_id=1, source_target_pairs={{248,0},{0,8},{8,16},{16,24},{24,32},{32,40},{40,48},{48,56},{56,6... | collective-permute-start | bytes 786440 | tf_op jit(solution)/shard_map/while/body/eval_jaxpr/ppermute | solution.py:12
  437.4 20.9 %collective-permute-start = (f32[4,128,128]{2,0,1:T(4,128)S(1)}, f32[4,128,128]{2,0,1:T(4,128)S(1)}, u32[]{:S(2)}, u32[]{:S(2)}) collective-permute-start(f32[4,128,128]{2,0,1:T(4,128)S(1)} %get-tuple-element.235), channel_id=1, source_target_pairs={{248,0},{0,8},{8,16},{16,24},{24,32},{32,40},{40,48},{48,56},{56,6... | collective-permute-start | bytes 786440 | tf_op jit(solution)/shard_map/while/body/eval_jaxpr/ppermute | solution.py:12
  459.2 18.4 %collective-permute-start = (f32[4,128,128]{2,0,1:T(4,128)S(1)}, f32[4,128,128]{2,0,1:T(4,128)S(1)}, u32[]{:S(2)}, u32[]{:S(2)}) collective-permute-start(f32[4,128,128]{2,0,1:T(4,128)S(1)} %get-tuple-element.235), channel_id=1, source_target_pairs={{248,0},{0,8},{8,16},{16,24},{24,32},{32,40},{40,48},{48,56},{56,6... | collective-permute-start | bytes 786440 | tf_op jit(solution)/shard_map/while/body/eval_jaxpr/ppermute | solution.py:12
  478.5 15.2 %collective-permute-start = (f32[4,128,128]{2,0,1:T(4,128)S(1)}, f32[4,128,128]{2,0,1:T(4,128)S(1)}, u32[]{:S(2)}, u32[]{:S(2)}) collective-permute-start(f32[4,128,128]{2,0,1:T(4,128)S(1)} %get-tuple-element.235), channel_id=1, source_target_pairs={{248,0},{0,8},{8,16},{16,24},{24,32},{32,40},{40,48},{48,56},{56,6... | collective-permute-start | bytes 786440 | tf_op jit(solution)/shard_map/while/body/eval_jaxpr/ppermute | solution.py:12
  494.6 20.6 %collective-permute-start = (f32[4,128,128]{2,0,1:T(4,128)S(1)}, f32[4,128,128]{2,0,1:T(4,128)S(1)}, u32[]{:S(2)}, u32[]{:S(2)}) collective-permute-start(f32[4,128,128]{2,0,1:T(4,128)S(1)} %get-tuple-element.235), channel_id=1, source_target_pairs={{248,0},{0,8},{8,16},{16,24},{24,32},{32,40},{40,48},{48,56},{56,6... | collective-permute-start | bytes 786440 | tf_op jit(solution)/shard_map/while/body/eval_jaxpr/ppermute | solution.py:12
  516.1 18.8 %collective-permute-start = (f32[4,128,128]{2,0,1:T(4,128)S(1)}, f32[4,128,128]{2,0,1:T(4,128)S(1)}, u32[]{:S(2)}, u32[]{:S(2)}) collective-permute-start(f32[4,128,128]{2,0,1:T(4,128)S(1)} %get-tuple-element.235), channel_id=1, source_target_pairs={{248,0},{0,8},{8,16},{16,24},{24,32},{32,40},{40,48},{48,56},{56,6... | collective-permute-start | bytes 786440 | tf_op jit(solution)/shard_map/while/body/eval_jaxpr/ppermute | solution.py:12
  535.9 18.1 %collective-permute-start = (f32[4,128,128]{2,0,1:T(4,128)S(1)}, f32[4,128,128]{2,0,1:T(4,128)S(1)}, u32[]{:S(2)}, u32[]{:S(2)}) collective-permute-start(f32[4,128,128]{2,0,1:T(4,128)S(1)} %get-tuple-element.235), channel_id=1, source_target_pairs={{248,0},{0,8},{8,16},{16,24},{24,32},{32,40},{40,48},{48,56},{56,6... | collective-permute-start | bytes 786440 | tf_op jit(solution)/shard_map/while/body/eval_jaxpr/ppermute | solution.py:12
  554.9 20.0 %collective-permute-start = (f32[4,128,128]{2,0,1:T(4,128)S(1)}, f32[4,128,128]{2,0,1:T(4,128)S(1)}, u32[]{:S(2)}, u32[]{:S(2)}) collective-permute-start(f32[4,128,128]{2,0,1:T(4,128)S(1)} %get-tuple-element.235), channel_id=1, source_target_pairs={{248,0},{0,8},{8,16},{16,24},{24,32},{32,40},{40,48},{48,56},{56,6... | collective-permute-start | bytes 786440 | tf_op jit(solution)/shard_map/while/body/eval_jaxpr/ppermute | solution.py:12
  575.8 16.0 %collective-permute-start = (f32[4,128,128]{2,0,1:T(4,128)S(1)}, f32[4,128,128]{2,0,1:T(4,128)S(1)}, u32[]{:S(2)}, u32[]{:S(2)}) collective-permute-start(f32[4,128,128]{2,0,1:T(4,128)S(1)} %get-tuple-element.235), channel_id=1, source_target_pairs={{248,0},{0,8},{8,16},{16,24},{24,32},{32,40},{40,48},{48,56},{56,6... | collective-permute-start | bytes 786440 | tf_op jit(solution)/shard_map/while/body/eval_jaxpr/ppermute | solution.py:12
  592.7 13.4 %collective-permute-start = (f32[4,128,128]{2,0,1:T(4,128)S(1)}, f32[4,128,128]{2,0,1:T(4,128)S(1)}, u32[]{:S(2)}, u32[]{:S(2)}) collective-permute-start(f32[4,128,128]{2,0,1:T(4,128)S(1)} %get-tuple-element.235), channel_id=1, source_target_pairs={{248,0},{0,8},{8,16},{16,24},{24,32},{32,40},{40,48},{48,56},{56,6... | collective-permute-start | bytes 786440 | tf_op jit(solution)/shard_map/while/body/eval_jaxpr/ppermute | solution.py:12
  607.0 13.4 %collective-permute-start = (f32[4,128,128]{2,0,1:T(4,128)S(1)}, f32[4,128,128]{2,0,1:T(4,128)S(1)}, u32[]{:S(2)}, u32[]{:S(2)}) collective-permute-start(f32[4,128,128]{2,0,1:T(4,128)S(1)} %get-tuple-element.235), channel_id=1, source_target_pairs={{248,0},{0,8},{8,16},{16,24},{24,32},{32,40},{40,48},{48,56},{56,6... | collective-permute-start | bytes 786440 | tf_op jit(solution)/shard_map/while/body/eval_jaxpr/ppermute | solution.py:12
  621.3 13.4 %collective-permute-start = (f32[4,128,128]{2,0,1:T(4,128)S(1)}, f32[4,128,128]{2,0,1:T(4,128)S(1)}, u32[]{:S(2)}, u32[]{:S(2)}) collective-permute-start(f32[4,128,128]{2,0,1:T(4,128)S(1)} %get-tuple-element.235), channel_id=1, source_target_pairs={{248,0},{0,8},{8,16},{16,24},{24,32},{32,40},{40,48},{48,56},{56,6... | collective-permute-start | bytes 786440 | tf_op jit(solution)/shard_map/while/body/eval_jaxpr/ppermute | solution.py:12
  635.6 13.4 %collective-permute-start = (f32[4,128,128]{2,0,1:T(4,128)S(1)}, f32[4,128,128]{2,0,1:T(4,128)S(1)}, u32[]{:S(2)}, u32[]{:S(2)}) collective-permute-start(f32[4,128,128]{2,0,1:T(4,128)S(1)} %get-tuple-element.235), channel_id=1, source_target_pairs={{248,0},{0,8},{8,16},{16,24},{24,32},{32,40},{40,48},{48,56},{56,6... | collective-permute-start | bytes 786440 | tf_op jit(solution)/shard_map/while/body/eval_jaxpr/ppermute | solution.py:12
  (3 other events, 17.3 us)
